TPU v7x, 512 devices: a whole 4x4x16 slice. The times are simulated.
512 devices in a mesh: seq: 128 (over z, x, core), fsdp: 4 (over y).
Axes of the slice: x: 4, y: 4, z: 16, core: 2. Of those that a mesh axis runs over, the one named last changes fastest.
Arguments:
- query_key: bfloat16 [131072, 3072], P(('seq', 'fsdp')), may hold values from -48 to 48
- values: bfloat16 [131072, 3072], P(('seq', 'fsdp')), may hold values from -6 to 6
- cluster_ids: int32 [24, 1024], replicated, may hold values from 0 to 127, as said below
Outputs:
- attended: bfloat16 [131072, 3072], P(('seq', 'fsdp'))
Inputs may be any that keep to these rules, and one draw needn't show every extreme that they name: `cluster_ids`: for every head and cluster at most 10 blocks name that cluster, and for every head some cluster is named by exactly 10 blocks. Among the (head, block) pairs of one group of 6 consecutive heads and one run of 8 blocks starting at a multiple of 8, no cluster is named more than 1 times, and some cluster exactly 1 times; the blocks of one such run name distinct clusters for each head.
All inputs are finite; a program needn't handle non-finite values.
Results may differ from a plain program's by a relative error of at most 0.0027.
Values may be sent and summed in bfloat16 or wider, within the bound.
No kernel may reach another device: no remote copies, remote signals or barrier semaphores. Data moves between devices by JAX's collectives and lax.ppermute only.
A program may use at most 64 MiB of HBM per device.

v0:
```python
import math
import jax
import jax.numpy as jnp
from jax import lax
from jax.sharding import PartitionSpec as P

BLK = 128
masked_score = -1e30


def by_index(source_table, row_index):
    padded = jnp.concatenate(
        [source_table, jnp.zeros((1,) + source_table.shape[1:], source_table.dtype)], axis=0
    )
    return padded[row_index]


def softmax_group(key_rows, positions, alive_rows, score_scale):
    half = BLK // 2
    blocks = key_rows.shape[0] // BLK

    def by_half(rows):
        shaped = rows.reshape((blocks, 2, half) + rows.shape[1:])
        return jnp.swapaxes(shaped, 0, 1).reshape(rows.shape)

    query_rows = by_half(key_rows)
    query_positions = by_half(positions)
    query_alive = by_half(alive_rows)
    scores = jnp.dot(query_rows, key_rows.T, preferred_element_type=jnp.float32) * score_scale
    allowed = alive_rows[None, :] & (positions[None, :] <= query_positions[:, None])
    scores = jnp.where(allowed, scores, masked_score)
    row_peak = jnp.max(scores, axis=1, keepdims=True)
    weights = jnp.where(allowed, jnp.exp(scores - row_peak), 0.0)
    row_total = jnp.where(query_alive[:, None], jnp.sum(weights, axis=1, keepdims=True), 1.0)
    weights = weights.astype(jnp.bfloat16).reshape(2, blocks * half, key_rows.shape[0])
    row_total = row_total.reshape(2, blocks * half, 1)
    return (weights[0], weights[1], row_total[0], row_total[1])


def shards(query_key, values, cluster_ids):
    seq_count = lax.axis_size("seq")
    group_count = lax.axis_size("fsdp")
    seq_index = lax.axis_index("seq")
    group_index = lax.axis_index("fsdp")
    heads_all = cluster_ids.shape[0]
    group_heads = heads_all // group_count
    head_dim = query_key.shape[1] // heads_all
    tok_rows = query_key.shape[0]
    shard_blocks = group_count * tok_rows // BLK
    all_blocks = cluster_ids.shape[1]
    item_count = group_heads * shard_blocks
    slot_count = max(1, item_count // seq_count)
    capacity = shard_blocks + min(shard_blocks // 4, seq_count - shard_blocks)
    group_rows = capacity * BLK
    send_rows = seq_count * slot_count
    score_scale = 1.0 / math.sqrt(head_dim)
    keys_local, values_local = (
        lax.all_to_all(query_key, "fsdp", split_axis=1, concat_axis=0, tiled=True),
        lax.all_to_all(values, "fsdp", split_axis=1, concat_axis=0, tiled=True),
    )

    def into_items(block_data):
        shaped = block_data.reshape(shard_blocks, BLK, group_heads, head_dim)
        return jnp.transpose(shaped, (2, 0, 1, 3)).reshape(item_count, BLK, head_dim)

    key_items = into_items(keys_local)
    value_items = into_items(values_local)
    group_ids = lax.dynamic_slice_in_dim(cluster_ids, group_index * group_heads, group_heads, 0)
    by_source = jnp.transpose(
        group_ids.reshape(group_heads, seq_count, shard_blocks), (1, 0, 2)
    ).reshape(seq_count, item_count)
    own_dest = lax.dynamic_index_in_dim(by_source, seq_index, 0, keepdims=False)
    item_ids = jnp.arange(item_count, dtype=jnp.int32)
    earlier = (own_dest[None, :] == own_dest[:, None]) & (item_ids[None, :] < item_ids[:, None])
    own_pos = own_dest * slot_count + jnp.sum(earlier.astype(jnp.int32), axis=1)
    row_ids = jnp.arange(send_rows, dtype=jnp.int32)
    slot_match = own_pos[None, :] == row_ids[:, None]
    send_pick = jnp.sum(jnp.where(slot_match, item_ids[None, :], 0), axis=1) + item_count * (
        1 - jnp.any(slot_match, axis=1).astype(jnp.int32)
    )
    received_mask = (by_source == seq_index).astype(jnp.int32)
    recv_pos = (
        jnp.arange(seq_count, dtype=jnp.int32)[:, None] * slot_count
        + jnp.cumsum(received_mask, axis=1)
        - received_mask
    )
    recv_by_head = jnp.transpose(
        recv_pos.reshape(seq_count, group_heads, shard_blocks), (1, 0, 2)
    ).reshape(group_heads * all_blocks)
    owned_mask = (group_ids == seq_index).astype(jnp.int32)
    ordinal = jnp.cumsum(owned_mask, axis=1) - owned_mask
    target = jnp.where(
        owned_mask > 0, jnp.arange(group_heads, dtype=jnp.int32)[:, None] * capacity + ordinal, -1
    ).reshape(group_heads * all_blocks)
    slot_ids = jnp.arange(group_heads * capacity, dtype=jnp.int32)
    matches = target[None, :] == slot_ids[:, None]
    present = jnp.any(matches, axis=1)
    source_row = jnp.sum(jnp.where(matches, recv_by_head[None, :], 0), axis=1) + send_rows * (
        1 - present.astype(jnp.int32)
    )
    block_ids = jnp.tile(jnp.arange(all_blocks, dtype=jnp.int32), group_heads)
    block_of = jnp.sum(jnp.where(matches, block_ids[None, :], 0), axis=1)
    arrived_k = lax.all_to_all(
        by_index(key_items, send_pick), "seq", split_axis=0, concat_axis=0, tiled=True
    )
    arrived_v = lax.all_to_all(
        by_index(value_items, send_pick), "seq", split_axis=0, concat_axis=0, tiled=True
    )
    key_grouped = by_index(arrived_k, source_row)
    value_grouped = by_index(arrived_v, source_row)
    positions = (block_of[:, None] * BLK + jnp.arange(BLK, dtype=jnp.int32)[None, :]).reshape(
        group_heads, group_rows
    )
    alive_rows = jnp.repeat(present, BLK).reshape(group_heads, group_rows)

    def one_head(operands):
        key_rows, where_at, alive_here = operands
        return softmax_group(key_rows, where_at, alive_here, score_scale)

    weights_0, weights_1, totals_0, totals_1 = lax.map(
        one_head, (key_grouped.reshape(group_heads, group_rows, head_dim), positions, alive_rows)
    )
    half = BLK // 2
    value_rows = value_grouped.reshape(group_heads, group_rows, head_dim)
    back_match = source_row[None, :] == row_ids[:, None]
    back_pick = jnp.sum(
        jnp.where(back_match, slot_ids[None, :], 0), axis=1
    ) + group_heads * capacity * (1 - jnp.any(back_match, axis=1).astype(jnp.int32))
    pieces = []
    for part in range(2):
        part_weights = (weights_0, weights_1)[part]
        weighted = jnp.einsum(
            "hqk,hkd->hqd", part_weights, value_rows, preferred_element_type=jnp.float32
        )
        part_total = (totals_0, totals_1)[part]
        outputs = (weighted / part_total).astype(jnp.bfloat16)
        outputs = outputs.reshape(group_heads * capacity, half, head_dim)
        returned = lax.all_to_all(
            by_index(outputs, back_pick), "seq", split_axis=0, concat_axis=0, tiled=True
        )
        own_output = by_index(returned, own_pos)
        token_major = jnp.transpose(
            own_output.reshape(group_heads, shard_blocks, half, head_dim), (1, 2, 0, 3)
        ).reshape(shard_blocks * half, group_heads * head_dim)
        pieces.append(lax.all_to_all(token_major, "fsdp", split_axis=0, concat_axis=1, tiled=True))
    own_blocks = tok_rows // BLK
    joined = jnp.stack(
        [piece.reshape(own_blocks, half, heads_all * head_dim) for piece in pieces], axis=1
    )
    return joined.reshape(tok_rows, heads_all * head_dim)


def solution(mesh):
    placed = (P(("seq", "fsdp"), None), P(("seq", "fsdp"), None), P())
    return jax.shard_map(
        shards, mesh=mesh, in_specs=placed, out_specs=P(("seq", "fsdp"), None), check_vma=False
    )
```

profile of v0, /device:TPU:32, one launch (start us, length us, event | category | flops | bytes accessed | tf_op | source)
XLA Modules:
  0.0 725.8 jit_solution(8790920589746454872)
XLA Ops:
  0.0 2.6 copy.104
  2.6 4.6 all-to-all-start
  20.4 7.5 %all-to-all-done = bf16[256,4,768]{0,2,1:T(8,128)(2,1)S(1)} async-done(((bf16[256,4,768]{0,2,1:T(8,128)(2,1)}), bf16[256,4,768]{0,2,1:T(8,128)(2,1)S(1)}, u32[]{:S(2)}, u32[]{:S(2)}) %all-to-all-start) | async-done | bytes 1572896 | tf_op jit(solution)/shard_map/all_to_all | solution.py:58
  27.9 3.6 all-to-all-start.2
  34.8 2.5 reshape.280
  40.7 3.1 gather_fusion
  43.8 7.5 %all-to-all-done.2 = bf16[256,4,768]{0,2,1:T(8,128)(2,1)S(1)} async-done(((bf16[256,4,768]{0,2,1:T(8,128)(2,1)}), bf16[256,4,768]{0,2,1:T(8,128)(2,1)S(1)}, u32[]{:S(2)}, u32[]{:S(2)}) %all-to-all-start.2) | async-done | bytes 1572896 | tf_op jit(solution)/shard_map/all_to_all | solution.py:59
  51.3 19.5 %all-to-all-start.1 = ((bf16[128,128,128]{2,1,0:T(8,128)(2,1)}), bf16[128,128,128]{2,1,0:T(8,128)(2,1)}, u32[]{:S(2)}, u32[]{:S(2)}) async-start(bf16[128,128,128]{2,1,0:T(8,128)(2,1)} %gather_fusion), calls=%async_computation.1 | async-start | bytes 8388608 | tf_op jit(solution)/shard_map/all_to_all | solution.py:103
  76.1 3.1 gather_fusion.2
  79.2 179.2 %all-to-all-done.1 = bf16[128,128,128]{2,1,0:T(8,128)(2,1)} async-done(((bf16[128,128,128]{2,1,0:T(8,128)(2,1)}), bf16[128,128,128]{2,1,0:T(8,128)(2,1)}, u32[]{:S(2)}, u32[]{:S(2)}) %all-to-all-start.1) | async-done | bytes 4194336 | tf_op jit(solution)/shard_map/all_to_all | solution.py:103
  258.4 9.4 %all-to-all-start.3 = ((bf16[128,128,128]{2,1,0:T(8,128)(2,1)}), bf16[128,128,128]{2,1,0:T(8,128)(2,1)}, u32[]{:S(2)}, u32[]{:S(2)}) async-start(bf16[128,128,128]{2,1,0:T(8,128)(2,1)} %gather_fusion.2), calls=%async_computation.3 | async-start | bytes 8388608 | tf_op jit(solution)/shard_map/all_to_all | solution.py:106
  268.3 5.8 concatenate.25
  274.1 3.1 gather_fusion.1
  277.3 41.2 %while.16 = (s32[]{:T(128)}, bf16[6,640,1280]{1,2,0:T(8,128)(2,1)}, bf16[6,640,1280]{1,2,0:T(8,128)(2,1)}, f32[6,640,1]{1,0,2:T(8,128)S(1)}, f32[6,640,1]{1,0,2:...) while((s32[]{:T(128)}, bf16[6,640,1280]{1,2,0:T(8,128)(2,1)}, ...), condition=%wide.region_12.13_spmd, body=%wide.region_9.12_spmd.sunk | while | flops 437451520 | bytes 25025912 | solution.py:120
  279.3 2.4 fusion.30
  286.2 2.4 fusion.30
  293.1 2.4 fusion.30
  299.9 2.4 fusion.30
  306.8 2.4 fusion.30
  318.5 137.1 %all-to-all-done.3 = bf16[128,128,128]{2,1,0:T(8,128)(2,1)} async-done(((bf16[128,128,128]{2,1,0:T(8,128)(2,1)}), bf16[128,128,128]{2,1,0:T(8,128)(2,1)}, u32[]{:S(2)}, u32[]{:S(2)}) %all-to-all-start.3) | async-done | bytes 4194336 | tf_op jit(solution)/shard_map/all_to_all | solution.py:106
  455.5 5.8 concatenate.27
  461.3 3.1 gather_fusion.3
  464.5 7.7 %divide_convert_fusion.1 = bf16[6,640,128]{2,1,0:T(8,128)(2,1)S(1)} fusion(f32[6,640]{1,0:T(8,128)S(1)} %bitcast.151, bf16[6,640,1280]{1,2,0:T(8,128)(2,1)} %get-tuple-element.50, bf16[6,1280,128]{2,1,0:T(8,128)(2,1)S(1)} %bitcast.140), kind=kOutput, calls=%fused_computation.26 | convolution fusion | flops 1259274240 | bytes 12794880 | tf_op jit(solution)/shard_map/hqk,hkd->hqd/dot_general | solution.py:132
  474.5 8.9 %all-to-all-start.4 = ((bf16[128,64,128]{2,1,0:T(8,128)(2,1)}), bf16[128,64,128]{2,1,0:T(8,128)(2,1)S(1)}, u32[]{:S(2)}, u32[]{:S(2)}) async-start(bf16[128,64,128]{2,1,0:T(8,128)(2,1)} %gather_fusion.4), calls=%async_computation.4 | async-start | bytes 4194304 | tf_op jit(solution)/shard_map/all_to_all | solution.py:138
  483.4 7.6 %divide_convert_fusion = bf16[6,640,128]{2,1,0:T(8,128)(2,1)S(1)} fusion(f32[6,640]{1,0:T(8,128)S(1)} %bitcast.152, bf16[6,640,1280]{1,2,0:T(8,128)(2,1)} %get-tuple-element.52, bf16[6,1280,128]{2,1,0:T(8,128)(2,1)} %bitcast.141), kind=kOutput, calls=%fused_computation.25 | convolution fusion | flops 1259274240 | bytes 12794880 | tf_op jit(solution)/shard_map/hqk,hkd->hqd/dot_general | solution.py:132
  493.2 88.5 %all-to-all-done.4 = bf16[128,64,128]{2,1,0:T(8,128)(2,1)S(1)} async-done(((bf16[128,64,128]{2,1,0:T(8,128)(2,1)}), bf16[128,64,128]{2,1,0:T(8,128)(2,1)S(1)}, u32[]{:S(2)}, u32[]{:S(2)}) %all-to-all-start.4) | async-done | bytes 2097184 | tf_op jit(solution)/shard_map/all_to_all | solution.py:138
  581.7 9.1 %all-to-all-start.6 = ((bf16[128,64,128]{2,1,0:T(8,128)(2,1)}), bf16[128,64,128]{2,1,0:T(8,128)(2,1)}, u32[]{:S(2)}, u32[]{:S(2)}) async-start(bf16[128,64,128]{2,1,0:T(8,128)(2,1)} %gather_fusion.6), calls=%async_computation.6 | async-start | bytes 4194304 | tf_op jit(solution)/shard_map/all_to_all | solution.py:138
  597.3 91.5 %all-to-all-done.6 = bf16[128,64,128]{2,1,0:T(8,128)(2,1)} async-done(((bf16[128,64,128]{2,1,0:T(8,128)(2,1)}), bf16[128,64,128]{2,1,0:T(8,128)(2,1)}, u32[]{:S(2)}, u32[]{:S(2)}) %all-to-all-start.6) | async-done | bytes 2097184 | tf_op jit(solution)/shard_map/all_to_all | solution.py:138
  688.8 4.2 all-to-all-start.5
  698.0 8.4 %all-to-all-done.5 = bf16[4,128,768]{2,1,0:T(8,128)(2,1)} async-done(((bf16[4,128,768]{2,1,0:T(8,128)(2,1)}), bf16[4,128,768]{2,1,0:T(8,128)(2,1)}, u32[]{:S(2)}, u32[]{:S(2)}) %all-to-all-start.5) | async-done | bytes 786464 | tf_op jit(solution)/shard_map/all_to_all | solution.py:145
  706.5 3.7 all-to-all-start.7
  712.5 10.5 %all-to-all-done.7 = bf16[4,128,768]{2,1,0:T(8,128)(2,1)S(1)} async-done(((bf16[4,128,768]{2,1,0:T(8,128)(2,1)}), bf16[4,128,768]{2,1,0:T(8,128)(2,1)S(1)}, u32[]{:S(2)}, u32[]{:S(2)}) %all-to-all-start.7) | async-done | bytes 786464 | tf_op jit(solution)/shard_map/all_to_all | solution.py:145
  (180 shorter events, 75.1 us)
Async XLA Ops:
  2.6 15.8 %copy-start.1 = (bf16[256,3072]{1,0:T(8,128)(2,1)S(1)}, bf16[256,3072]{1,0:T(8,128)(2,1)}, u32[]{:S(2)}) copy-start(bf16[256,3072]{1,0:T(8,128)(2,1)} %param.6) | copy-start | bytes 4718596
  2.6 25.3 %all-to-all-start = ((bf16[256,4,768]{0,2,1:T(8,128)(2,1)}), bf16[256,4,768]{0,2,1:T(8,128)(2,1)S(1)}, u32[]{:S(2)}, u32[]{:S(2)}) async-start(bf16[256,4,768]{0,2,1:T(8,128)(2,1)} %bitcast.13), calls=%async_computation | async-start | bytes 3145728 | tf_op jit(solution)/shard_map/all_to_all | solution.py:58
  17.1 2.9 copy-start.2
  17.1 3.1 copy-start.3
  20.0 11.5 %copy-start.4 = (s32[6144]{0:T(1024)S(1)}, s32[6144]{0:T(1024)}, u32[]{:S(2)}) copy-start(s32[6144]{0:T(1024)} %broadcast_in_dim.110) | copy-start | bytes 73732
  27.9 23.4 %all-to-all-start.2 = ((bf16[256,4,768]{0,2,1:T(8,128)(2,1)}), bf16[256,4,768]{0,2,1:T(8,128)(2,1)S(1)}, u32[]{:S(2)}, u32[]{:S(2)}) async-start(bf16[256,4,768]{0,2,1:T(8,128)(2,1)} %bitcast.132), calls=%async_computation.2 | async-start | bytes 3145728 | tf_op jit(solution)/shard_map/all_to_all | solution.py:59
  51.3 207.2 %all-to-all-start.1 = ((bf16[128,128,128]{2,1,0:T(8,128)(2,1)}), bf16[128,128,128]{2,1,0:T(8,128)(2,1)}, u32[]{:S(2)}, u32[]{:S(2)}) async-start(bf16[128,128,128]{2,1,0:T(8,128)(2,1)} %gather_fusion), calls=%async_computation.1 | async-start | bytes 8388608 | tf_op jit(solution)/shard_map/all_to_all | solution.py:103
  258.4 197.1 %all-to-all-start.3 = ((bf16[128,128,128]{2,1,0:T(8,128)(2,1)}), bf16[128,128,128]{2,1,0:T(8,128)(2,1)}, u32[]{:S(2)}, u32[]{:S(2)}) async-start(bf16[128,128,128]{2,1,0:T(8,128)(2,1)} %gather_fusion.2), calls=%async_computation.3 | async-start | bytes 8388608 | tf_op jit(solution)/shard_map/all_to_all | solution.py:106
  464.5 7.8 %copy-start = (bf16[60,128,128]{2,1,0:T(8,128)(2,1)}, bf16[60,128,128]{2,1,0:T(8,128)(2,1)S(1)}, u32[]{:S(2)}) copy-start(bf16[60,128,128]{2,1,0:T(8,128)(2,1)S(1)} %gather_fusion.3) | copy-start | bytes 5898244
  474.5 107.2 %all-to-all-start.4 = ((bf16[128,64,128]{2,1,0:T(8,128)(2,1)}), bf16[128,64,128]{2,1,0:T(8,128)(2,1)S(1)}, u32[]{:S(2)}, u32[]{:S(2)}) async-start(bf16[128,64,128]{2,1,0:T(8,128)(2,1)} %gather_fusion.4), calls=%async_computation.4 | async-start | bytes 4194304 | tf_op jit(solution)/shard_map/all_to_all | solution.py:138
  581.7 107.1 %all-to-all-start.6 = ((bf16[128,64,128]{2,1,0:T(8,128)(2,1)}), bf16[128,64,128]{2,1,0:T(8,128)(2,1)}, u32[]{:S(2)}, u32[]{:S(2)}) async-start(bf16[128,64,128]{2,1,0:T(8,128)(2,1)} %gather_fusion.6), calls=%async_computation.6 | async-start | bytes 4194304 | tf_op jit(solution)/shard_map/all_to_all | solution.py:138
  688.8 17.7 %all-to-all-start.5 = ((bf16[4,128,768]{2,1,0:T(8,128)(2,1)}), bf16[4,128,768]{2,1,0:T(8,128)(2,1)}, u32[]{:S(2)}, u32[]{:S(2)}) async-start(bf16[4,128,768]{2,1,0:T(8,128)(2,1)} %all_to_all.69), calls=%async_computation.5 | async-start | bytes 1572864 | tf_op jit(solution)/shard_map/all_to_all | solution.py:145
  706.5 16.5 %all-to-all-start.7 = ((bf16[4,128,768]{2,1,0:T(8,128)(2,1)}), bf16[4,128,768]{2,1,0:T(8,128)(2,1)S(1)}, u32[]{:S(2)}, u32[]{:S(2)}) async-start(bf16[4,128,768]{2,1,0:T(8,128)(2,1)} %all_to_all.73), calls=%async_computation.7 | async-start | bytes 1572864 | tf_op jit(solution)/shard_map/all_to_all | solution.py:145
where the time goes:
time: 735 us; the launch traced here: 726 us
  waiting for transfers between devices  530 us (72%)
  local copies, waits for them, and re-layouts  83.8 us (11%)
  starting transfers between devices  62.9 us (9%)
  matrix products  25.9 us (4%)
  other arithmetic  22 us (3%)
    all_to_all x2, waiting for transfers between devices, shards(): lax.all_to_all(by_index(outputs, back_pick), 'seq', split_axis=0, concat_...  180 us
    all_to_all x1, waiting for transfers between devices, shards(): lax.all_to_all(by_index(key_items, send_pick), 'seq', split_axis=0, conca...  179 us
    all_to_all x1, waiting for transfers between devices, shards(): lax.all_to_all(by_index(value_items, send_pick), 'seq', split_axis=0, con...  137 us
    gather x8, local copies, waits for them, and re-layouts, by_index(): return padded[row_index]  19.8 us
    all_to_all x1, starting transfers between devices, shards(): lax.all_to_all(by_index(key_items, send_pick), 'seq', split_axis=0, conca...  19.5 us
    all_to_all x2, waiting for transfers between devices, shards(): lax.all_to_all(token_major, 'fsdp', split_axis=0, concat_axis=1, tiled=True)  18.9 us
    concatenate x8, local copies, waits for them, and re-layouts, by_index(): jnp.concatenate([source_table, jnp.zeros((1,) + source_table.shape[1:], s...  18.7 us
    all_to_all x2, starting transfers between devices, shards(): lax.all_to_all(by_index(outputs, back_pick), 'seq', split_axis=0, concat_...  18 us
  transfers between devices with their start and end apart: 8, of which 8 were waited for; matrix products, arithmetic and copies ran while one was open for 14% of the time, Pallas kernels for 0%

commit v1 on v0

--- a/solution.py
+++ b/solution.py
@@ -6,6 +6,22 @@
 
 BLK = 128
 masked_score = -1e30
+
+
+def pairwise_exchange(x, axis, split, join):
+    ways, here = (lax.axis_size(axis), lax.axis_index(axis))
+    width = x.shape[split] // ways
+    shape = list(x.shape)
+    shape[split] = width
+    height = shape[join]
+    shape[join] = height * ways
+    full = jnp.zeros(shape, x.dtype)
+    for mask in range(ways):
+        part = lax.dynamic_slice_in_dim(x, (here ^ mask) * width, width, axis=split)
+        if mask:
+            part = lax.ppermute(part, axis, [(d, d ^ mask) for d in range(ways)])
+        full = lax.dynamic_update_slice_in_dim(full, part, (here ^ mask) * height, axis=join)
+    return full
 
 
 def by_index(source_table, row_index):
@@ -142,7 +158,7 @@
         token_major = jnp.transpose(
             own_output.reshape(group_heads, shard_blocks, half, head_dim), (1, 2, 0, 3)
         ).reshape(shard_blocks * half, group_heads * head_dim)
-        pieces.append(lax.all_to_all(token_major, "fsdp", split_axis=0, concat_axis=1, tiled=True))
+        pieces.append(pairwise_exchange(token_major, "fsdp", 0, 1))
     own_blocks = tok_rows // BLK
     joined = jnp.stack(
         [piece.reshape(own_blocks, half, heads_all * head_dim) for piece in pieces], axis=1

time: 735 us -> 726 us (0.988); the launches traced: 726 us -> 724 us
  waiting for transfers between devices: 530 us -> 519 us
  starting transfers between devices: 62.9 us -> 73.3 us
    all_to_all x2 -> x0, waiting for transfers between devices: 18.9 us -> none  [shards(): lax.all_to_all(token_major, 'fsdp', split_axis=0, concat_axis=1, tiled=True)]
    ppermute x0 -> x6, starting transfers between devices: none -> 18.7 us  [pairwise_exchange(): part = lax.ppermute(part, axis, [(d, d ^ mask) for d in range(ways)])]
    ppermute x0 -> x6, waiting for transfers between devices: none -> 10.9 us  [pairwise_exchange(): part = lax.ppermute(part, axis, [(d, d ^ mask) for d in range(ways)])]
    all_to_all x2 -> x0, starting transfers between devices: 7.9 us -> none  [shards(): lax.all_to_all(token_major, 'fsdp', split_axis=0, concat_axis=1, tiled=True)]
  transfers between devices with their start and end apart: 8 -> 12, of which waited for: 8 -> 9; matrix products, arithmetic and copies ran while one was open for 14% -> 15% of each run, Pallas kernels for 0% -> 0%
where the time goes in v1:
time: 726 us; the launch traced here: 724 us
  waiting for transfers between devices  519 us (71%)
  local copies, waits for them, and re-layouts  81.8 us (11%)
  starting transfers between devices  73.3 us (10%)
  matrix products  25.9 us (4%)
  other arithmetic  23.1 us (3%)
    all_to_all x1, waiting for transfers between devices, shards(): lax.all_to_all(by_index(key_items, send_pick), 'seq', split_axis=0, conca...  179 us
    all_to_all x2, waiting for transfers between devices, shards(): lax.all_to_all(by_index(outputs, back_pick), 'seq', split_axis=0, concat_...  177 us
    all_to_all x1, waiting for transfers between devices, shards(): lax.all_to_all(by_index(value_items, send_pick), 'seq', split_axis=0, con...  137 us
    gather x8, local copies, waits for them, and re-layouts, by_index(): return padded[row_index]  21.4 us
    concatenate x8, local copies, waits for them, and re-layouts, by_index(): jnp.concatenate([source_table, jnp.zeros((1,) + source_table.shape[1:], s...  20 us
    all_to_all x1, starting transfers between devices, shards(): lax.all_to_all(by_index(key_items, send_pick), 'seq', split_axis=0, conca...  19.5 us
    ppermute x6, starting transfers between devices, pairwise_exchange(): part = lax.ppermute(part, axis, [(d, d ^ mask) for d in range(ways)])  18.7 us
    all_to_all x2, starting transfers between devices, shards(): lax.all_to_all(by_index(outputs, back_pick), 'seq', split_axis=0, concat_...  17.5 us
  transfers between devices with their start and end apart: 12, of which 9 were waited for; matrix products, arithmetic and copies ran while one was open for 15% of the time, Pallas kernels for 0%

profile of v1, /device:TPU:32, one launch (start us, length us, event | category | flops | bytes accessed | tf_op | source)
XLA Modules:
  0.0 724.3 jit_solution(8244968038627660337)
XLA Ops:
  0.0 2.6 copy.81
  2.6 4.6 all-to-all-start
  20.4 7.5 %all-to-all-done = bf16[256,4,768]{0,2,1:T(8,128)(2,1)S(1)} async-done(((bf16[256,4,768]{0,2,1:T(8,128)(2,1)}), bf16[256,4,768]{0,2,1:T(8,128)(2,1)S(1)}, u32[]{:S(2)}, u32[]{:S(2)}) %all-to-all-start) | async-done | bytes 1572896 | tf_op jit(solution)/shard_map/all_to_all | solution.py:74
  27.9 3.6 all-to-all-start.2
  34.8 2.5 reshape.274
  40.7 3.1 gather_fusion
  43.8 7.5 %all-to-all-done.2 = bf16[256,4,768]{0,2,1:T(8,128)(2,1)S(1)} async-done(((bf16[256,4,768]{0,2,1:T(8,128)(2,1)}), bf16[256,4,768]{0,2,1:T(8,128)(2,1)S(1)}, u32[]{:S(2)}, u32[]{:S(2)}) %all-to-all-start.2) | async-done | bytes 1572896 | tf_op jit(solution)/shard_map/all_to_all | solution.py:75
  51.3 19.5 %all-to-all-start.1 = ((bf16[128,128,128]{2,1,0:T(8,128)(2,1)}), bf16[128,128,128]{2,1,0:T(8,128)(2,1)}, u32[]{:S(2)}, u32[]{:S(2)}) async-start(bf16[128,128,128]{2,1,0:T(8,128)(2,1)} %gather_fusion), calls=%async_computation.1 | async-start | bytes 8388608 | tf_op jit(solution)/shard_map/all_to_all | solution.py:119
  76.1 3.1 gather_fusion.2
  79.2 179.2 %all-to-all-done.1 = bf16[128,128,128]{2,1,0:T(8,128)(2,1)} async-done(((bf16[128,128,128]{2,1,0:T(8,128)(2,1)}), bf16[128,128,128]{2,1,0:T(8,128)(2,1)}, u32[]{:S(2)}, u32[]{:S(2)}) %all-to-all-start.1) | async-done | bytes 4194336 | tf_op jit(solution)/shard_map/all_to_all | solution.py:119
  258.4 9.4 %all-to-all-start.3 = ((bf16[128,128,128]{2,1,0:T(8,128)(2,1)}), bf16[128,128,128]{2,1,0:T(8,128)(2,1)}, u32[]{:S(2)}, u32[]{:S(2)}) async-start(bf16[128,128,128]{2,1,0:T(8,128)(2,1)} %gather_fusion.2), calls=%async_computation.3 | async-start | bytes 8388608 | tf_op jit(solution)/shard_map/all_to_all | solution.py:122
  268.3 5.8 concatenate.25
  274.1 3.1 gather_fusion.1
  277.3 41.2 %while.16 = (s32[]{:T(128)}, bf16[6,640,1280]{1,2,0:T(8,128)(2,1)}, bf16[6,640,1280]{1,2,0:T(8,128)(2,1)}, f32[6,640,1]{1,0,2:T(8,128)S(1)}, f32[6,640,1]{1,0,2:...) while((s32[]{:T(128)}, bf16[6,640,1280]{1,2,0:T(8,128)(2,1)}, ...), condition=%wide.region_12.13_spmd, body=%wide.region_9.12_spmd.sunk | while | flops 437451520 | bytes 25025912 | solution.py:136
  299.9 2.4 fusion.30
  318.5 137.1 %all-to-all-done.3 = bf16[128,128,128]{2,1,0:T(8,128)(2,1)} async-done(((bf16[128,128,128]{2,1,0:T(8,128)(2,1)}), bf16[128,128,128]{2,1,0:T(8,128)(2,1)}, u32[]{:S(2)}, u32[]{:S(2)}) %all-to-all-start.3) | async-done | bytes 4194336 | tf_op jit(solution)/shard_map/all_to_all | solution.py:122
  455.5 5.8 concatenate.27
  461.3 3.1 gather_fusion.3
  464.5 7.7 %divide_convert_fusion.1 = bf16[6,640,128]{2,1,0:T(8,128)(2,1)S(1)} fusion(f32[6,640]{1,0:T(8,128)S(1)} %bitcast.168, bf16[6,640,1280]{1,2,0:T(8,128)(2,1)} %get-tuple-element.50, bf16[6,1280,128]{2,1,0:T(8,128)(2,1)S(1)} %bitcast.157), kind=kOutput, calls=%fused_computation.26 | convolution fusion | flops 1259274240 | bytes 12794880 | tf_op jit(solution)/shard_map/hqk,hkd->hqd/dot_general | solution.py:148
  474.5 8.9 %all-to-all-start.4 = ((bf16[128,64,128]{2,1,0:T(8,128)(2,1)}), bf16[128,64,128]{2,1,0:T(8,128)(2,1)S(1)}, u32[]{:S(2)}, u32[]{:S(2)}) async-start(bf16[128,64,128]{2,1,0:T(8,128)(2,1)} %gather_fusion.4), calls=%async_computation.4 | async-start | bytes 4194304 | tf_op jit(solution)/shard_map/all_to_all | solution.py:154
  483.4 7.6 %divide_convert_fusion = bf16[6,640,128]{2,1,0:T(8,128)(2,1)S(1)} fusion(f32[6,640]{1,0:T(8,128)S(1)} %bitcast.169, bf16[6,640,1280]{1,2,0:T(8,128)(2,1)} %get-tuple-element.52, bf16[6,1280,128]{2,1,0:T(8,128)(2,1)} %bitcast.158), kind=kOutput, calls=%fused_computation.25 | convolution fusion | flops 1259274240 | bytes 12794880 | tf_op jit(solution)/shard_map/hqk,hkd->hqd/dot_general | solution.py:148
  493.2 88.5 %all-to-all-done.4 = bf16[128,64,128]{2,1,0:T(8,128)(2,1)S(1)} async-done(((bf16[128,64,128]{2,1,0:T(8,128)(2,1)}), bf16[128,64,128]{2,1,0:T(8,128)(2,1)S(1)}, u32[]{:S(2)}, u32[]{:S(2)}) %all-to-all-start.4) | async-done | bytes 2097184 | tf_op jit(solution)/shard_map/all_to_all | solution.py:154
  583.1 8.6 %all-to-all-start.5 = ((bf16[128,64,128]{2,1,0:T(8,128)(2,1)}), bf16[128,64,128]{2,1,0:T(8,128)(2,1)S(1)}, u32[]{:S(2)}, u32[]{:S(2)}) async-start(bf16[128,64,128]{2,1,0:T(8,128)(2,1)} %gather_fusion.6), calls=%async_computation.5 | async-start | bytes 4194304 | tf_op jit(solution)/shard_map/all_to_all | solution.py:154
  591.7 3.4 concatenate.29
  598.9 2.5 collective-permute-start
  601.4 88.6 %all-to-all-done.5 = bf16[128,64,128]{2,1,0:T(8,128)(2,1)S(1)} async-done(((bf16[128,64,128]{2,1,0:T(8,128)(2,1)}), bf16[128,64,128]{2,1,0:T(8,128)(2,1)S(1)}, u32[]{:S(2)}, u32[]{:S(2)}) %all-to-all-start.5) | async-done | bytes 2097184 | tf_op jit(solution)/shard_map/all_to_all | solution.py:154
  695.7 2.5 collective-permute-start.3
  698.2 4.0 collective-permute-start.1
  702.2 4.0 collective-permute-start.2
  708.1 3.9 collective-permute-start.5
  712.1 4.9 collective-permute-done.4
  718.8 4.2 collective-permute-done.5
  (195 shorter events, 84.2 us)
Async XLA Ops:
  2.6 15.8 %copy-start.2 = (bf16[256,3072]{1,0:T(8,128)(2,1)S(1)}, bf16[256,3072]{1,0:T(8,128)(2,1)}, u32[]{:S(2)}) copy-start(bf16[256,3072]{1,0:T(8,128)(2,1)} %param.6) | copy-start | bytes 4718596
  2.6 25.3 %all-to-all-start = ((bf16[256,4,768]{0,2,1:T(8,128)(2,1)}), bf16[256,4,768]{0,2,1:T(8,128)(2,1)S(1)}, u32[]{:S(2)}, u32[]{:S(2)}) async-start(bf16[256,4,768]{0,2,1:T(8,128)(2,1)} %bitcast.13), calls=%async_computation | async-start | bytes 3145728 | tf_op jit(solution)/shard_map/all_to_all | solution.py:74
  17.1 2.9 copy-start.3
  17.1 3.1 copy-start.4
  20.0 11.5 %copy-start.5 = (s32[6144]{0:T(1024)S(1)}, s32[6144]{0:T(1024)}, u32[]{:S(2)}) copy-start(s32[6144]{0:T(1024)} %broadcast_in_dim.110) | copy-start | bytes 73732
  27.9 23.4 %all-to-all-start.2 = ((bf16[256,4,768]{0,2,1:T(8,128)(2,1)}), bf16[256,4,768]{0,2,1:T(8,128)(2,1)S(1)}, u32[]{:S(2)}, u32[]{:S(2)}) async-start(bf16[256,4,768]{0,2,1:T(8,128)(2,1)} %bitcast.144), calls=%async_computation.2 | async-start | bytes 3145728 | tf_op jit(solution)/shard_map/all_to_all | solution.py:75
  51.3 207.2 %all-to-all-start.1 = ((bf16[128,128,128]{2,1,0:T(8,128)(2,1)}), bf16[128,128,128]{2,1,0:T(8,128)(2,1)}, u32[]{:S(2)}, u32[]{:S(2)}) async-start(bf16[128,128,128]{2,1,0:T(8,128)(2,1)} %gather_fusion), calls=%async_computation.1 | async-start | bytes 8388608 | tf_op jit(solution)/shard_map/all_to_all | solution.py:119
  258.4 197.1 %all-to-all-start.3 = ((bf16[128,128,128]{2,1,0:T(8,128)(2,1)}), bf16[128,128,128]{2,1,0:T(8,128)(2,1)}, u32[]{:S(2)}, u32[]{:S(2)}) async-start(bf16[128,128,128]{2,1,0:T(8,128)(2,1)} %gather_fusion.2), calls=%async_computation.3 | async-start | bytes 8388608 | tf_op jit(solution)/shard_map/all_to_all | solution.py:122
  464.5 7.8 %copy-start.1 = (bf16[60,128,128]{2,1,0:T(8,128)(2,1)}, bf16[60,128,128]{2,1,0:T(8,128)(2,1)S(1)}, u32[]{:S(2)}) copy-start(bf16[60,128,128]{2,1,0:T(8,128)(2,1)S(1)} %gather_fusion.3) | copy-start | bytes 5898244
  474.5 107.2 %all-to-all-start.4 = ((bf16[128,64,128]{2,1,0:T(8,128)(2,1)}), bf16[128,64,128]{2,1,0:T(8,128)(2,1)S(1)}, u32[]{:S(2)}, u32[]{:S(2)}) async-start(bf16[128,64,128]{2,1,0:T(8,128)(2,1)} %gather_fusion.4), calls=%async_computation.4 | async-start | bytes 4194304 | tf_op jit(solution)/shard_map/all_to_all | solution.py:154
  581.7 1.3 copy-start
  583.1 107.0 %all-to-all-start.5 = ((bf16[128,64,128]{2,1,0:T(8,128)(2,1)}), bf16[128,64,128]{2,1,0:T(8,128)(2,1)S(1)}, u32[]{:S(2)}, u32[]{:S(2)}) async-start(bf16[128,64,128]{2,1,0:T(8,128)(2,1)} %gather_fusion.6), calls=%async_computation.5 | async-start | bytes 4194304 | tf_op jit(solution)/shard_map/all_to_all | solution.py:154
  598.9 109.1 %collective-permute-start = (bf16[128,768]{1,0:T(8,128)(2,1)}, bf16[128,768]{1,0:T(8,128)(2,1)S(1)}, u32[]{:S(2)}, u32[]{:S(2)}) collective-permute-start(bf16[128,768]{1,0:T(8,128)(2,1)} %get-tuple-element.87), channel_id=1, source_target_pairs={{0,1},{1,0},{2,3},{3,2},{4,5},{5,4},{6,7},{7,6},{8,9},{9,8},{10,11... | collective-permute-start | bytes 589832 | tf_op jit(solution)/shard_map/ppermute | solution.py:22
  695.7 16.4 %collective-permute-start.3 = (bf16[128,768]{1,0:T(8,128)(2,1)}, bf16[128,768]{1,0:T(8,128)(2,1)S(1)}, u32[]{:S(2)}, u32[]{:S(2)}) collective-permute-start(bf16[128,768]{1,0:T(8,128)(2,1)} %get-tuple-element.91), channel_id=1, source_target_pairs={{0,1},{1,0},{2,3},{3,2},{4,5},{5,4},{6,7},{7,6},{8,9},{9,8},{10,11... | collective-permute-start | bytes 589832 | tf_op jit(solution)/shard_map/ppermute | solution.py:22
  698.2 13.9 %collective-permute-start.1 = (bf16[128,768]{1,0:T(8,128)(2,1)S(1)}, bf16[128,768]{1,0:T(8,128)(2,1)S(1)}, u32[]{:S(2)}, u32[]{:S(2)}) collective-permute-start(bf16[128,768]{1,0:T(8,128)(2,1)S(1)} %get-tuple-element.86), channel_id=1, source_target_pairs={{0,2},{1,3},{2,0},{3,1},{4,6},{5,7},{6,4},{7,5},{8,10},{9,11},{10,... | collective-permute-start | bytes 589832 | tf_op jit(solution)/shard_map/ppermute | solution.py:22
  702.2 16.7 %collective-permute-start.2 = (bf16[128,768]{1,0:T(8,128)(2,1)S(1)}, bf16[128,768]{1,0:T(8,128)(2,1)S(1)}, u32[]{:S(2)}, u32[]{:S(2)}) collective-permute-start(bf16[128,768]{1,0:T(8,128)(2,1)S(1)} %get-tuple-element.85), channel_id=1, source_target_pairs={{0,3},{1,2},{2,1},{3,0},{4,7},{5,6},{6,5},{7,4},{8,11},{9,10},{10,... | collective-permute-start | bytes 589832 | tf_op jit(solution)/shard_map/ppermute | solution.py:22
  706.1 10.9 %collective-permute-start.4 = (bf16[128,768]{1,0:T(8,128)(2,1)}, bf16[128,768]{1,0:T(8,128)(2,1)S(1)}, u32[]{:S(2)}, u32[]{:S(2)}) collective-permute-start(bf16[128,768]{1,0:T(8,128)(2,1)} %get-tuple-element.90), channel_id=1, source_target_pairs={{0,2},{1,3},{2,0},{3,1},{4,6},{5,7},{6,4},{7,5},{8,10},{9,11},{10,... | collective-permute-start | bytes 589832 | tf_op jit(solution)/shard_map/ppermute | solution.py:22
  708.1 14.9 %collective-permute-start.5 = (bf16[128,768]{1,0:T(8,128)(2,1)S(1)}, bf16[128,768]{1,0:T(8,128)(2,1)S(1)}, u32[]{:S(2)}, u32[]{:S(2)}) collective-permute-start(bf16[128,768]{1,0:T(8,128)(2,1)S(1)} %get-tuple-element.89), channel_id=1, source_target_pairs={{0,3},{1,2},{2,1},{3,0},{4,7},{5,6},{6,5},{7,4},{8,11},{9,10},{10,... | collective-permute-start | bytes 589832 | tf_op jit(solution)/shard_map/ppermute | solution.py:22
